TPU v7x, 128 devices: a whole 4x4x4 slice. The times are simulated.
128 devices in a mesh: row: 8 (over y, core), col: 16 (over x, z).
Axes of the slice: x: 4, y: 4, z: 4, core: 2. Of those that a mesh axis runs over, the one named last changes fastest.
Arguments:
- occ_coeffs: bfloat16 [49152, 20480], P('row', 'col'), may hold values from -0.21875 to 0.21875
- colloc: bfloat16 [1024, 1024, 512], P(('row', 'col')), may hold values from -6 to 6
- grid_points: float32 [1024, 3, 512], P(('row', 'col')), may hold values from -4 to 4
- grid_weights: float32 [1024, 512], P(('row', 'col')), may hold values from 0.01 to 0.1
- charge_sites: float32 [3, 512], replicated, may hold values from -4 to 4
- charge_proj: bfloat16 [512, 128], replicated, may hold values from -0.5 to 0.5
- shell_lists: int32 [1024, 16], P(('row', 'col')), may hold values from 0 to 767, as said below
- point_counts: int32 [1024], P(('row', 'col')), may hold values from 1 to 512, as said below
Outputs:
- exchange_slab: float32 [49152, 128], P(('row', 'col'))
Inputs may be any that keep to these rules, and one draw needn't show every extreme that they name: `shell_lists`: batches b * 8 to b * 8 + 7 belong to the b-th device in row+col order, and the blocks named by one device's batches are all different. Owner device o holds blocks o * 6 to o * 6 + 5; one device's batches name at most 2 blocks of one owner, and in every draw one owner gets exactly 2 from every device. `point_counts`: points of a batch beyond its count are not part of it.
All inputs are finite; a program needn't handle non-finite values.
Results may differ from a plain program's by a relative error of at most 0.0045.
Values may be sent and summed in bfloat16 or wider, within the bound.
No kernel may reach another device: no remote copies, remote signals or barrier semaphores. Data moves between devices by JAX's collectives and lax.ppermute only.
A program may use at most 128 MiB of HBM per device.

v0:
```python
import jax
import jax.numpy as jnp
from jax import lax
from jax.sharding import PartitionSpec as P

SH = 64
NSIG = 16
smear_sq = 0.25


def broadcast_from_first(value, axis):
    size = lax.axis_size(axis)
    index = lax.axis_index(axis)
    have = 1
    while have < size:
        pairs = [(src, src + have) for src in range(have) if src + have < size]
        moved = lax.ppermute(value, axis, pairs)
        value = jnp.where(index >= have, moved, value)
        have *= 2
    return value


def potential(points, charge_sites):
    dist_sq = (points[:, 0][:, None, :] - charge_sites[0][None, :, None]) ** 2
    dist_sq = dist_sq + (points[:, 1][:, None, :] - charge_sites[1][None, :, None]) ** 2
    dist_sq = dist_sq + (points[:, 2][:, None, :] - charge_sites[2][None, :, None]) ** 2
    return lax.rsqrt(dist_sq + smear_sq)


def batch_terms(
    dens_rows, colloc, grid_points, grid_weights, charge_sites, charge_proj, point_counts
):
    total_points = colloc.shape[2]
    field = jnp.einsum(
        "bfs,bfp->bsp", dens_rows, colloc, preferred_element_type=jnp.float32
    ).astype(jnp.bfloat16)
    projected = jnp.einsum("ks,bsp->bkp", charge_proj, field, preferred_element_type=jnp.float32)
    live = (jnp.arange(total_points)[None, :] < point_counts[:, None]).astype(jnp.float32)
    charges = (
        projected * potential(grid_points, charge_sites) * (grid_weights * live)[:, None, :]
    ).astype(jnp.bfloat16)
    spread_back = jnp.einsum(
        "ks,bkp->bsp", charge_proj, charges, preferred_element_type=jnp.float32
    ).astype(jnp.bfloat16)
    return jnp.einsum("bfp,bsp->bfs", colloc, spread_back, preferred_element_type=jnp.float32)


def on_device(
    occ_coeffs,
    colloc,
    grid_points,
    grid_weights,
    charge_sites,
    charge_proj,
    shell_lists,
    point_counts,
):
    row_count = lax.axis_size("row")
    col_count = lax.axis_size("col")
    owners = row_count * col_count
    me = lax.axis_index("row") * col_count + lax.axis_index("col")
    group_rows = occ_coeffs.shape[0]
    slab_width = charge_proj.shape[1]
    own_rows = group_rows // col_count
    own_blocks = own_rows // SH
    tile = SH * slab_width
    all_lists = lax.all_gather(shell_lists, ("row", "col"), tiled=True)
    window = broadcast_from_first(occ_coeffs[:slab_width], "row")
    requested = shell_lists.reshape(-1)
    request_count = requested.shape[0]
    capacity = 2 * request_count // owners
    slots = owners * capacity
    owner = requested // own_blocks
    onehot = (owner[:, None] == jnp.arange(owners)[None, :]).astype(jnp.int32)
    before = jnp.cumsum(onehot, axis=0) - onehot
    rank = jnp.sum(before * onehot, axis=1)
    slot = owner * capacity + rank
    pick = (slot[:, None] == jnp.arange(slots)[None, :]).astype(jnp.bfloat16)
    lists = all_lists.reshape(owners, request_count)
    mine = (lists // own_blocks == me).astype(jnp.int32)
    order = jnp.cumsum(mine, axis=1)
    local = lists % own_blocks
    wanted_by = []
    for place in range(capacity):
        hit = mine * (order == place + 1)
        wanted_by.append(jnp.sum(hit * (local + 1), axis=1) - 1)
    received_ids = jnp.stack(wanted_by, axis=1).reshape(-1)
    serve = (received_ids[:, None] == jnp.arange(own_blocks)[None, :]).astype(jnp.bfloat16)
    density = lax.psum_scatter(
        lax.dot_general(
            occ_coeffs, window, (((1,), (1,)), ((), ())), preferred_element_type=jnp.float32
        ),
        "col",
        scatter_dimension=0,
        tiled=True,
    ).astype(jnp.bfloat16)
    store = density.reshape(own_blocks, tile)
    found = jnp.dot(serve, store, preferred_element_type=jnp.float32).astype(jnp.bfloat16)
    replies = lax.all_to_all(
        found.reshape(owners, capacity, tile),
        ("row", "col"),
        split_axis=0,
        concat_axis=0,
        tiled=True,
    )
    fetched = jnp.dot(
        pick, replies.reshape(slots, tile), preferred_element_type=jnp.float32
    ).astype(jnp.bfloat16)
    dens_rows = fetched.reshape(shell_lists.shape[0], NSIG * SH, slab_width)
    terms = batch_terms(
        dens_rows, colloc, grid_points, grid_weights, charge_sites, charge_proj, point_counts
    )
    terms = terms.astype(jnp.bfloat16).reshape(request_count, tile)
    tiles = lax.dot_general(
        pick, terms, (((0,), (0,)), ((), ())), preferred_element_type=jnp.float32
    ).astype(jnp.bfloat16)
    arrived = lax.all_to_all(
        tiles.reshape(owners, capacity, tile),
        ("row", "col"),
        split_axis=0,
        concat_axis=0,
        tiled=True,
    )
    summed = lax.dot_general(
        serve,
        arrived.reshape(slots, tile),
        (((0,), (0,)), ((), ())),
        preferred_element_type=jnp.float32,
    )
    return summed.reshape(own_rows, slab_width)


def solution(mesh):
    placed = (
        P("row", "col"),
        P(("row", "col"), None, None),
        P(("row", "col"), None, None),
        P(("row", "col"), None),
        P(),
        P(),
        P(("row", "col"), None),
        P(("row", "col")),
    )
    return jax.shard_map(
        on_device, mesh=mesh, in_specs=placed, out_specs=P(("row", "col"), None), check_vma=False
    )
```

profile of v0, /device:TPU:1, one launch (start us, length us, event | category | flops | bytes accessed | tf_op | source)
XLA Modules:
  0.0 319.2 jit_solution(13722545505886730577)
XLA Ops:
  6.5 1.0 slice.21
  7.6 1.3 collective-permute-start
  8.9 2.5 collective-permute-done
  11.4 1.0 broadcast_select_fusion
  12.4 1.3 collective-permute-start.1
  13.7 6.8 %collective-permute-done.1 = bf16[128,1280]{1,0:T(8,128)(2,1)S(1)} collective-permute-done((bf16[128,1280]{1,0:T(8,128)(2,1)S(1)}, bf16[128,1280]{1,0:T(8,128)(2,1)S(1)}, u32[]{:S(2)}, u32[]{:S(2)}) %collective-permute-start.1) | collective-permute-done | bytes 327712 | tf_op jit(solution)/shard_map/ppermute | solution.py:17
  20.5 1.3 collective-permute-start.2
  21.9 6.1 %collective-permute-done.2 = bf16[128,1280]{1,0:T(8,128)(2,1)S(1)} collective-permute-done((bf16[128,1280]{1,0:T(8,128)(2,1)S(1)}, bf16[128,1280]{1,0:T(8,128)(2,1)S(1)}, u32[]{:S(2)}, u32[]{:S(2)}) %collective-permute-start.2) | collective-permute-done | bytes 327712 | tf_op jit(solution)/shard_map/ppermute | solution.py:17
  28.0 12.3 %convolution_bitcast_fusion = f32[6144,128]{0,1:T(8,128)} fusion(bf16[6144,1280]{1,0:T(8,128)(2,1)} %param.8, bf16[128,1280]{1,0:T(8,128)(2,1)S(1)} %collective-permute-done.2, bf16[128,1280]{1,0:T(8,128)(2,1)S(1)} %broadcast_select_fusion.1, pred[]{:T(512)S(6)} %ge.9), kind=kOutput, calls=%fused_computation.6 | convolution fusion | flops 2013429760 | bytes 19529728 | tf_op jit(solution)/shard_map/dot_general | solution.py:90
  40.3 61.2 %all_gather.3 = s32[1024,16]{1,0:T(8,128)S(1)} all-gather(s32[8,16]{1,0:T(8,128)S(1)} %copy-done.3), channel_id=1, replica_groups=mesh['row'=8,'col'=16] {'row','col'}, dimensions={0}, use_global_device_ids=true | all-gather | bytes 66048 | tf_op jit(solution)/shard_map/all_gather | solution.py:67
  101.5 0.1 broadcast_divide_fusion
  101.7 0.2 div.28
  101.9 0.3 fusion.15
  102.2 0.2 and.32
  102.6 0.2 reduce_window_sum.22
  102.8 0.1 copy.13
  102.9 0.2 eq.75
  103.1 0.1 copy.14
  103.3 0.2 eq.80
  103.5 0.9 fusion.10
  104.5 0.1 reduce_sum.36
  104.7 0.1 reduce_sum.46
  104.8 0.1 copy.15
  104.9 0.1 eq.81
  105.1 17.2 %reduce-scatter.2.cloned.1.call-done = f32[384,128]{0,1:T(8,128)} async-done(((f32[6144,128]{0,1:T(8,128)}), f32[384,128]{0,1:T(8,128)}) %reduce-scatter.2.cloned.1.call-update) | async-done | bytes 196624 | tf_op jit(solution)/shard_map/reduce_scatter | solution.py:89
  122.2 0.9 convert_element_type.46
  123.2 0.1 copy.16
  123.3 0.1 reshape.107
  123.4 3.2 %convolution_convert_fusion.1 = bf16[256,8192]{1,0:T(8,128)(2,1)} fusion(bf16[6,8192]{1,0:T(8,128)(2,1)S(1)} %reshape.107, s32[256]{0:T(256)S(1)} %eq.81), kind=kOutput, calls=%fused_computation.1 | convolution fusion | flops 27264512 | bytes 4293632 | tf_op jit(solution)/shard_map/dot_general | solution.py:98
  126.7 7.6 %reshape.108 = bf16[128,2,8192]{2,1,0:T(2,128)(2,1)} reshape(bf16[256,8192]{1,0:T(8,128)(2,1)} %convolution_convert_fusion.1) | data formatting | bytes 8388608 | tf_op jit(solution)/shard_map/reshape | solution.py:100
  134.3 9.6 %all-to-all-start = ((bf16[128,2,8192]{2,1,0:T(2,128)(2,1)}), bf16[128,2,8192]{2,1,0:T(2,128)(2,1)}, u32[]{:S(2)}, u32[]{:S(2)}) async-start(bf16[128,2,8192]{2,1,0:T(2,128)(2,1)} %reshape.108), calls=%async_computation.1 | async-start | bytes 8388608 | tf_op jit(solution)/shard_map/all_to_all | solution.py:99
  144.2 0.2 reduce_window_sum.23
  144.4 0.2 select_reduce_fusion
  144.7 51.3 %all-to-all-done = bf16[128,2,8192]{2,1,0:T(2,128)(2,1)} async-done(((bf16[128,2,8192]{2,1,0:T(2,128)(2,1)}), bf16[128,2,8192]{2,1,0:T(2,128)(2,1)}, u32[]{:S(2)}, u32[]{:S(2)}) %all-to-all-start) | async-done | bytes 4194336 | tf_op jit(solution)/shard_map/all_to_all | solution.py:99
  196.0 7.2 %reshape.109 = bf16[256,8192]{1,0:T(8,128)(2,1)} reshape(bf16[128,2,8192]{2,1,0:T(2,128)(2,1)} %all-to-all-done) | data formatting | bytes 8388608 | tf_op jit(solution)/shard_map/reshape | solution.py:107
  203.2 4.3 %convolution_convert_fusion.2 = bf16[128,8192]{1,0:T(8,128)(2,1)} fusion(bf16[256,8192]{1,0:T(8,128)(2,1)} %reshape.109, s32[128]{0:T(128)S(1)} %multiply_add_fusion), kind=kOutput, calls=%fused_computation.2 | convolution fusion | flops 537952256 | bytes 6291968 | tf_op jit(solution)/shard_map/dot_general | solution.py:106
  207.5 2.9 reshape.110
  210.4 4.8 %convolution_convert_fusion.3 = bf16[8,128,512]{2,1,0:T(8,128)(2,1)S(1)} fusion(bf16[8,1024,128]{2,1,0:T(8,128)(2,1)S(1)} %reshape.110, bf16[8,1024,512]{2,1,0:T(8,128)(2,1)} %param.9), kind=kOutput, calls=%fused_computation.11 | convolution fusion | flops 1074266112 | bytes 11534336 | tf_op jit(solution)/shard_map/bfs,bfp->bsp/dot_general | solution.py:34
  215.2 5.9 %fusion.6 = bf16[8,512,128]{1,2,0:T(8,128)(2,1)} fusion(f32[8,512]{1,0:T(8,128)S(1)} %fusion.28, f32[512]{0:T(512)S(1)} %bitcast.41, f32[8,512]{1,0:T(8,128)S(1)} %get-tuple-element.10, f32[512]{0:T(512)S(1)} %bitcast.42, f32[8,512]{1,0:T(8,128)S(1)} %get-tuple-element.11, f32[512]{0:T(512)S(1)} %bitcast.40, f32[8,512]{1,0:T(8,128)S(1)} %get-tuple-element.9, ...), kind=kOutput, calls=%fused_computation.10 | convolution fusion | flops 1099431936 | bytes 2299904 | tf_op jit(solution)/shard_map/ks,bkp->bsp/dot_general | solution.py:42
  221.1 6.5 %convert_bitcast_fusion = bf16[8,1024,128]{1,2,0:T(8,128)(2,1)S(1)} fusion(bf16[8,512,128]{1,2,0:T(8,128)(2,1)} %fusion.6, bf16[8,1024,512]{2,1,0:T(8,128)(2,1)} %param.9), kind=kOutput, calls=%fused_computation.9 | convolution fusion | flops 1074790400 | bytes 11534336 | tf_op jit(solution)/shard_map/bfp,bsp->bfs/dot_general | solution.py:45
  227.6 2.4 copy.17
  230.0 2.8 reshape.111
  232.8 3.3 %convolution_convert_fusion = bf16[256,8192]{1,0:T(8,128)(2,1)} fusion(bf16[128,8192]{1,0:T(8,128)(2,1)S(1)} %reshape.111, s32[128]{0:T(128)S(1)} %multiply_add_fusion), kind=kOutput, calls=%fused_computation | convolution fusion | flops 539000832 | bytes 6291968 | tf_op jit(solution)/shard_map/dot_general | solution.py:114
  236.2 7.6 %reshape.112 = bf16[128,2,8192]{2,1,0:T(2,128)(2,1)} reshape(bf16[256,8192]{1,0:T(8,128)(2,1)} %convolution_convert_fusion) | data formatting | bytes 8388608 | tf_op jit(solution)/shard_map/reshape | solution.py:118
  243.8 57.6 %all_to_all.10 = bf16[128,2,8192]{2,1,0:T(2,128)(2,1)} all-to-all(bf16[128,2,8192]{2,1,0:T(2,128)(2,1)} %reshape.112), channel_id=1, replica_groups=mesh['row'=8,'col'=16] {'row','col'}, dimensions={0} | all-to-all | bytes 8388608 | tf_op jit(solution)/shard_map/all_to_all | solution.py:117
  301.4 7.2 %reshape.113 = bf16[256,8192]{1,0:T(8,128)(2,1)} reshape(bf16[128,2,8192]{2,1,0:T(2,128)(2,1)} %all_to_all.10) | data formatting | bytes 8388608 | tf_op jit(solution)/shard_map/reshape | solution.py:126
  308.6 2.9 fusion.20
  311.5 0.8 reshape.114
  (34 shorter events, 0.8 us)
Async XLA Ops:
  6.5 208.6 %copy-start = (bf16[512,128]{1,0:T(8,128)(2,1)S(1)}, bf16[512,128]{1,0:T(8,128)(2,1)}, u32[]{:S(2)}) copy-start(bf16[512,128]{1,0:T(8,128)(2,1)} %param.13) | copy-start | bytes 393220
  6.5 115.7 %reduce-scatter.2.cloned.1.call-start = ((), (), s32[]{:S(2)}) async-start(), calls=%async_computation.3 | async-start | bytes 3342336 | tf_op jit(solution)/shard_map/reduce_scatter | solution.py:89
  7.6 3.8 %collective-permute-start = (bf16[128,1280]{1,0:T(8,128)(2,1)S(1)}, bf16[128,1280]{1,0:T(8,128)(2,1)S(1)}, u32[]{:S(2)}, u32[]{:S(2)}) collective-permute-start(bf16[128,1280]{1,0:T(8,128)(2,1)S(1)} %slice.21), channel_id=1, source_target_pairs={{0,16},{1,17},{2,18},{3,19},{4,20},{5,21},{6,22},{7,23},{8,24},{9,... | collective-permute-start | bytes 983048 | tf_op jit(solution)/shard_map/ppermute | solution.py:17
  12.4 8.1 %collective-permute-start.1 = (bf16[128,1280]{1,0:T(8,128)(2,1)S(1)}, bf16[128,1280]{1,0:T(8,128)(2,1)S(1)}, u32[]{:S(2)}, u32[]{:S(2)}) collective-permute-start(bf16[128,1280]{1,0:T(8,128)(2,1)S(1)} %broadcast_select_fusion), channel_id=1, source_target_pairs={{0,32},{16,48},{1,33},{17,49},{2,34},{18,50},{3,35},{19,51},{4,36}... | collective-permute-start | bytes 983048 | tf_op jit(solution)/shard_map/ppermute | solution.py:17
  20.5 7.5 %collective-permute-start.2 = (bf16[128,1280]{1,0:T(8,128)(2,1)S(1)}, bf16[128,1280]{1,0:T(8,128)(2,1)S(1)}, u32[]{:S(2)}, u32[]{:S(2)}) collective-permute-start(bf16[128,1280]{1,0:T(8,128)(2,1)S(1)} %broadcast_select_fusion.1), channel_id=1, source_target_pairs={{0,64},{16,80},{32,96},{48,112},{1,65},{17,81},{33,97},{49,113},{2... | collective-permute-start | bytes 983048 | tf_op jit(solution)/shard_map/ppermute | solution.py:17
  21.8 18.5 %copy-start.3 = (s32[8,16]{1,0:T(8,128)S(1)}, s32[8,16]{1,0:T(8,128)}, u32[]{:S(2)}) copy-start(s32[8,16]{1,0:T(8,128)} %param.14) | copy-start | bytes 1540
  134.3 10.3 %copy-start.5 = (f32[3,512]{1,0:T(4,128)S(1)}, f32[3,512]{1,0:T(4,128)}, u32[]{:S(2)}) copy-start(f32[3,512]{1,0:T(4,128)} %param.12) | copy-start | bytes 18436
  134.3 10.3 %copy-start.4 = (f32[8,512]{1,0:T(8,128)S(1)}, f32[8,512]{1,0:T(8,128)}, u32[]{:S(2)}) copy-start(f32[8,512]{1,0:T(8,128)} %param.11) | copy-start | bytes 49156
  134.3 10.3 %copy-start.6 = (s32[8]{0:T(128)S(1)}, s32[8]{0:T(128)}, u32[]{:S(2)}) copy-start(s32[8]{0:T(128)} %param.15) | copy-start | bytes 100
  134.3 10.4 %copy-start.2 = (f32[8,3,512]{2,0,1:T(8,128)S(1)}, f32[8,3,512]{2,0,1:T(8,128)}, u32[]{:S(2)}) copy-start(f32[8,3,512]{2,0,1:T(8,128)} %param.10) | copy-start | bytes 147460
  134.3 61.7 %all-to-all-start = ((bf16[128,2,8192]{2,1,0:T(2,128)(2,1)}), bf16[128,2,8192]{2,1,0:T(2,128)(2,1)}, u32[]{:S(2)}, u32[]{:S(2)}) async-start(bf16[128,2,8192]{2,1,0:T(2,128)(2,1)} %reshape.108), calls=%async_computation.1 | async-start | bytes 8388608 | tf_op jit(solution)/shard_map/all_to_all | solution.py:99
  301.4 11.0 %copy-start.1 = (bf16[512,128]{1,0:T(8,128)(2,1)S(1)}, bf16[512,128]{1,0:T(8,128)(2,1)}, u32[]{:S(2)}) copy-start(bf16[512,128]{1,0:T(8,128)(2,1)} %param.13) | copy-start | bytes 393220
Sparse Core Ops, SparseCore 0:
  40.4 81.7 reduce-scatter.1
where the time goes:
time: 321 us; the launch traced here: 319 us
  blocking collectives  119 us (37%)
  waiting for transfers between devices  83.9 us (26%)
  matrix products  43.3 us (13%)
  local copies, waits for them, and re-layouts  41.7 us (13%)
  between operations  13.7 us (4%)
  starting transfers between devices  13.5 us (4%)
  other arithmetic  4.28 us (1%)
    all_gather x1, blocking collectives, on_device(): all_lists = lax.all_gather(shell_lists, ('row', 'col'), tiled=True)  61.2 us
    all_to_all x1, blocking collectives, on_device(): lax.all_to_all(tiles.reshape(owners, capacity, tile), ('row', 'col'), spl...  57.6 us
    all_to_all x1, waiting for transfers between devices, on_device(): lax.all_to_all(found.reshape(owners, capacity, tile), ('row', 'col'), spl...  51.3 us
    reduce_scatter x1, waiting for transfers between devices, on_device(): lax.psum_scatter(lax.dot_general(occ_coeffs, window, (((1,), (1,)), ((),...  17.2 us
    ppermute x3, waiting for transfers between devices, broadcast_from_first(): moved = lax.ppermute(value, axis, pairs)  15.4 us
    dot_general x1, matrix products, on_device(): lax.dot_general(occ_coeffs, window, (((1,), (1,)), ((), ())), preferred_e...  12.3 us
    all_to_all x1, starting transfers between devices, on_device(): lax.all_to_all(found.reshape(owners, capacity, tile), ('row', 'col'), spl...  9.57 us
    reshape x1, local copies, waits for them, and re-layouts, on_device(): found.reshape(owners, capacity, tile)  7.62 us
  transfers between devices with their start and end apart: 5, of which 5 were waited for; matrix products, arithmetic and copies ran while one was open for 1% of the time, Pallas kernels for 0%

commit v1 on v0

--- a/solution.py
+++ b/solution.py
@@ -64,7 +64,10 @@
     own_rows = group_rows // col_count
     own_blocks = own_rows // SH
     tile = SH * slab_width
-    all_lists = lax.all_gather(shell_lists, ("row", "col"), tiled=True)
+    peers = lax.axis_size(("row", "col"))
+    blocks = jnp.stack([shell_lists for _ in range(peers)])
+    blocks = lax.all_to_all(blocks, ("row", "col"), split_axis=0, concat_axis=0)
+    all_lists = jnp.concatenate(blocks, axis=0)
     window = broadcast_from_first(occ_coeffs[:slab_width], "row")
     requested = shell_lists.reshape(-1)
     request_count = requested.shape[0]

time: 321 us -> 320 us (level)
  blocking collectives: 119 us -> 57.6 us
  waiting for transfers between devices: 83.9 us -> 129 us
  starting transfers between devices: 13.5 us -> 28.6 us
    all_gather x1 -> x0, blocking collectives: 61.2 us -> none  [on_device(): all_lists = lax.all_gather(shell_lists, ('row', 'col'), tiled=True)]
    reduce_scatter x1, waiting for transfers between devices: 17.2 us -> 53.3 us  [on_device(): lax.psum_scatter(lax.dot_general(occ_coeffs, window, (((1,), (1,)), ((),...]
    all_to_all x0 -> x1, starting transfers between devices: none -> 15.1 us  [on_device(): blocks = lax.all_to_all(blocks, ('row', 'col'), split_axis=0, concat_axis=0)]
    all_to_all x0 -> x1, waiting for transfers between devices: none -> 9.47 us  [on_device(): blocks = lax.all_to_all(blocks, ('row', 'col'), split_axis=0, concat_axis=0)]
  transfers between devices with their start and end apart: 5 -> 6, of which waited for: 5 -> 6; matrix products, arithmetic and copies ran while one was open for 1% -> 1% of each run, Pallas kernels for 0% -> 0%
where the time goes in v1:
time: 320 us; the launch traced here: 318 us
  waiting for transfers between devices  129 us (40%)
  blocking collectives  57.6 us (18%)
  matrix products  43.2 us (14%)
  local copies, waits for them, and re-layouts  42.1 us (13%)
  starting transfers between devices  28.6 us (9%)
  between operations  13.7 us (4%)
  other arithmetic  3.73 us (1%)
    all_to_all x1, blocking collectives, on_device(): lax.all_to_all(tiles.reshape(owners, capacity, tile), ('row', 'col'), spl...  57.6 us
    reduce_scatter x1, waiting for transfers between devices, on_device(): lax.psum_scatter(lax.dot_general(occ_coeffs, window, (((1,), (1,)), ((),...  53.3 us
    all_to_all x1, waiting for transfers between devices, on_device(): lax.all_to_all(found.reshape(owners, capacity, tile), ('row', 'col'), spl...  51.3 us
    ppermute x3, waiting for transfers between devices, broadcast_from_first(): moved = lax.ppermute(value, axis, pairs)  15.4 us
    all_to_all x1, starting transfers between devices, on_device(): blocks = lax.all_to_all(blocks, ('row', 'col'), split_axis=0, concat_axis=0)  15.1 us
    dot_general x1, matrix products, on_device(): lax.dot_general(occ_coeffs, window, (((1,), (1,)), ((), ())), preferred_e...  12.3 us
    all_to_all x1, starting transfers between devices, on_device(): lax.all_to_all(found.reshape(owners, capacity, tile), ('row', 'col'), spl...  9.59 us
    all_to_all x1, waiting for transfers between devices, on_device(): blocks = lax.all_to_all(blocks, ('row', 'col'), split_axis=0, concat_axis=0)  9.47 us
  transfers between devices with their start and end apart: 6, of which 6 were waited for; matrix products, arithmetic and copies ran while one was open for 1% of the time, Pallas kernels for 0%

profile of v1, /device:TPU:1, one launch (start us, length us, event | category | flops | bytes accessed | tf_op | source)
XLA Modules:
  0.0 318.3 jit_solution(11947451546033048476)
XLA Ops:
  6.5 1.0 slice.21
  7.6 1.3 collective-permute-start
  8.9 2.5 collective-permute-done
  11.4 1.0 broadcast_select_fusion
  12.4 1.3 collective-permute-start.1
  13.7 6.8 %collective-permute-done.1 = bf16[128,1280]{1,0:T(8,128)(2,1)S(1)} collective-permute-done((bf16[128,1280]{1,0:T(8,128)(2,1)S(1)}, bf16[128,1280]{1,0:T(8,128)(2,1)S(1)}, u32[]{:S(2)}, u32[]{:S(2)}) %collective-permute-start.1) | collective-permute-done | bytes 327712 | tf_op jit(solution)/shard_map/ppermute | solution.py:17
  20.5 1.3 collective-permute-start.2
  21.9 6.1 %collective-permute-done.2 = bf16[128,1280]{1,0:T(8,128)(2,1)S(1)} collective-permute-done((bf16[128,1280]{1,0:T(8,128)(2,1)S(1)}, bf16[128,1280]{1,0:T(8,128)(2,1)S(1)}, u32[]{:S(2)}, u32[]{:S(2)}) %collective-permute-start.2) | collective-permute-done | bytes 327712 | tf_op jit(solution)/shard_map/ppermute | solution.py:17
  28.0 12.3 %convolution_bitcast_fusion = f32[6144,128]{0,1:T(8,128)} fusion(bf16[6144,1280]{1,0:T(8,128)(2,1)} %param.8, bf16[128,1280]{1,0:T(8,128)(2,1)S(1)} %collective-permute-done.2, bf16[128,1280]{1,0:T(8,128)(2,1)S(1)} %broadcast_select_fusion.1, pred[]{:T(512)S(6)} %ge.9), kind=kOutput, calls=%fused_computation.6 | convolution fusion | flops 2013429760 | bytes 19529728 | tf_op jit(solution)/shard_map/dot_general | solution.py:93
  40.3 0.9 reshape.115
  41.2 15.1 %all-to-all-start = ((s32[128,1,128]{2,1,0:T(1,128)}), s32[128,1,128]{2,1,0:T(1,128)S(1)}, u32[]{:S(2)}, u32[]{:S(2)}) async-start(s32[128,1,128]{2,1,0:T(1,128)} %reshape.115), calls=%async_computation | async-start | bytes 131072 | tf_op jit(solution)/shard_map/all_to_all | solution.py:69
  56.3 9.5 %all-to-all-done = s32[128,1,128]{2,1,0:T(1,128)S(1)} async-done(((s32[128,1,128]{2,1,0:T(1,128)}), s32[128,1,128]{2,1,0:T(1,128)S(1)}, u32[]{:S(2)}, u32[]{:S(2)}) %all-to-all-start) | async-done | bytes 65568 | tf_op jit(solution)/shard_map/all_to_all | solution.py:69
  65.8 0.5 broadcast.138
  66.3 0.8 reduce.2
  67.1 0.2 reshape.116
  67.3 0.2 copy.23
  67.6 0.2 reduce_window_sum.22
  67.8 0.1 fusion.15
  67.9 0.1 copy.26
  68.0 0.1 eq.81
  68.2 53.3 %reduce-scatter.2.cloned.1.call-done = f32[384,128]{0,1:T(8,128)} async-done(((f32[6144,128]{0,1:T(8,128)}), f32[384,128]{0,1:T(8,128)}) %reduce-scatter.2.cloned.1.call-update) | async-done | bytes 196624 | tf_op jit(solution)/shard_map/reduce_scatter | solution.py:92
  121.5 0.9 convert_element_type.46
  122.4 0.1 copy.27
  122.6 0.1 reshape.106
  122.7 3.2 %convolution_convert_fusion.1 = bf16[256,8192]{1,0:T(8,128)(2,1)} fusion(bf16[6,8192]{1,0:T(8,128)(2,1)S(1)} %reshape.106, s32[256]{0:T(256)S(1)} %eq.81), kind=kOutput, calls=%fused_computation.1 | convolution fusion | flops 27264512 | bytes 4293632 | tf_op jit(solution)/shard_map/dot_general | solution.py:101
  125.9 7.6 %reshape.107 = bf16[128,2,8192]{2,1,0:T(2,128)(2,1)} reshape(bf16[256,8192]{1,0:T(8,128)(2,1)} %convolution_convert_fusion.1) | data formatting | bytes 8388608 | tf_op jit(solution)/shard_map/reshape | solution.py:103
  133.6 9.6 %all-to-all-start.1 = ((bf16[128,2,8192]{2,1,0:T(2,128)(2,1)}), bf16[128,2,8192]{2,1,0:T(2,128)(2,1)}, u32[]{:S(2)}, u32[]{:S(2)}) async-start(bf16[128,2,8192]{2,1,0:T(2,128)(2,1)} %reshape.107), calls=%async_computation.2 | async-start | bytes 8388608 | tf_op jit(solution)/shard_map/all_to_all | solution.py:102
  143.2 0.1 div.30
  143.3 0.1 and.35
  143.4 0.1 fusion.23
  143.5 0.2 reduce_window_sum.23
  143.6 0.2 select_reduce_fusion
  143.9 0.1 fusion.28
  144.0 51.3 %all-to-all-done.1 = bf16[128,2,8192]{2,1,0:T(2,128)(2,1)} async-done(((bf16[128,2,8192]{2,1,0:T(2,128)(2,1)}), bf16[128,2,8192]{2,1,0:T(2,128)(2,1)}, u32[]{:S(2)}, u32[]{:S(2)}) %all-to-all-start.1) | async-done | bytes 4194336 | tf_op jit(solution)/shard_map/all_to_all | solution.py:102
  195.3 7.2 %reshape.108 = bf16[256,8192]{1,0:T(8,128)(2,1)} reshape(bf16[128,2,8192]{2,1,0:T(2,128)(2,1)} %all-to-all-done.1) | data formatting | bytes 8388608 | tf_op jit(solution)/shard_map/reshape | solution.py:110
  202.5 4.3 %convolution_convert_fusion.2 = bf16[128,8192]{1,0:T(8,128)(2,1)} fusion(bf16[256,8192]{1,0:T(8,128)(2,1)} %reshape.108, s32[128]{0:T(128)S(1)} %multiply_add_fusion), kind=kOutput, calls=%fused_computation.2 | convolution fusion | flops 537952256 | bytes 6291968 | tf_op jit(solution)/shard_map/dot_general | solution.py:109
  206.8 2.9 reshape.109
  209.6 4.8 %convolution_convert_fusion.3 = bf16[8,128,512]{2,1,0:T(8,128)(2,1)S(1)} fusion(bf16[8,1024,128]{2,1,0:T(8,128)(2,1)S(1)} %reshape.109, bf16[8,1024,512]{2,1,0:T(8,128)(2,1)} %param.9), kind=kOutput, calls=%fused_computation.11 | convolution fusion | flops 1074266112 | bytes 11534336 | tf_op jit(solution)/shard_map/bfs,bfp->bsp/dot_general | solution.py:34
  214.4 5.7 %fusion.6 = bf16[8,512,128]{2,1,0:T(8,128)(2,1)} fusion(f32[8,512]{1,0:T(8,128)S(1)} %fusion.28, f32[512]{0:T(512)S(1)} %bitcast.51, f32[8,512]{1,0:T(8,128)S(1)} %get-tuple-element.8, f32[512]{0:T(512)S(1)} %bitcast.52, f32[8,512]{1,0:T(8,128)S(1)} %get-tuple-element.9, f32[512]{0:T(512)S(1)} %bitcast.50, f32[8,512]{1,0:T(8,128)S(1)} %get-tuple-element.7, ...), kind=kOutput, calls=%fused_computation.10 | convolution fusion | flops 1099431936 | bytes 2299904 | tf_op jit(solution)/shard_map/ks,bkp->bsp/dot_general | solution.py:42
  220.2 6.6 %convert_bitcast_fusion = bf16[8,1024,128]{1,2,0:T(8,128)(2,1)S(1)} fusion(bf16[8,512,128]{2,1,0:T(8,128)(2,1)} %fusion.6, bf16[8,1024,512]{2,1,0:T(8,128)(2,1)} %param.9), kind=kOutput, calls=%fused_computation.9 | convolution fusion | flops 1074790400 | bytes 11534336 | tf_op jit(solution)/shard_map/bfp,bsp->bfs/dot_general | solution.py:45
  226.8 2.4 copy.31
  229.2 2.8 reshape.110
  232.0 3.3 %convolution_convert_fusion = bf16[256,8192]{1,0:T(8,128)(2,1)} fusion(bf16[128,8192]{1,0:T(8,128)(2,1)S(1)} %reshape.110, s32[128]{0:T(128)S(1)} %multiply_add_fusion), kind=kOutput, calls=%fused_computation | convolution fusion | flops 539000832 | bytes 6291968 | tf_op jit(solution)/shard_map/dot_general | solution.py:117
  235.3 7.6 %reshape.111 = bf16[128,2,8192]{2,1,0:T(2,128)(2,1)} reshape(bf16[256,8192]{1,0:T(8,128)(2,1)} %convolution_convert_fusion) | data formatting | bytes 8388608 | tf_op jit(solution)/shard_map/reshape | solution.py:121
  242.9 57.6 %all_to_all.15 = bf16[128,2,8192]{2,1,0:T(2,128)(2,1)} all-to-all(bf16[128,2,8192]{2,1,0:T(2,128)(2,1)} %reshape.111), channel_id=1, replica_groups=mesh['row'=8,'col'=16] {'row','col'}, dimensions={0} | all-to-all | bytes 8388608 | tf_op jit(solution)/shard_map/all_to_all | solution.py:120
  300.5 7.2 %reshape.112 = bf16[256,8192]{1,0:T(8,128)(2,1)} reshape(bf16[128,2,8192]{2,1,0:T(2,128)(2,1)} %all_to_all.15) | data formatting | bytes 8388608 | tf_op jit(solution)/shard_map/reshape | solution.py:129
  307.8 2.9 fusion.13
  310.7 0.8 reshape.113
  (29 shorter events, 0.3 us)
Async XLA Ops:
  6.5 207.9 %copy-start = (bf16[512,128]{1,0:T(8,128)(2,1)S(1)}, bf16[512,128]{1,0:T(8,128)(2,1)}, u32[]{:S(2)}) copy-start(bf16[512,128]{1,0:T(8,128)(2,1)} %param.13) | copy-start | bytes 393220
  6.5 115.0 %reduce-scatter.2.cloned.1.call-start = ((), (), s32[]{:S(2)}) async-start(), calls=%async_computation.4 | async-start | bytes 3342336 | tf_op jit(solution)/shard_map/reduce_scatter | solution.py:92
  7.6 3.8 %collective-permute-start = (bf16[128,1280]{1,0:T(8,128)(2,1)S(1)}, bf16[128,1280]{1,0:T(8,128)(2,1)S(1)}, u32[]{:S(2)}, u32[]{:S(2)}) collective-permute-start(bf16[128,1280]{1,0:T(8,128)(2,1)S(1)} %slice.21), channel_id=1, source_target_pairs={{0,16},{1,17},{2,18},{3,19},{4,20},{5,21},{6,22},{7,23},{8,24},{9,... | collective-permute-start | bytes 983048 | tf_op jit(solution)/shard_map/ppermute | solution.py:17
  12.4 8.1 %collective-permute-start.1 = (bf16[128,1280]{1,0:T(8,128)(2,1)S(1)}, bf16[128,1280]{1,0:T(8,128)(2,1)S(1)}, u32[]{:S(2)}, u32[]{:S(2)}) collective-permute-start(bf16[128,1280]{1,0:T(8,128)(2,1)S(1)} %broadcast_select_fusion), channel_id=1, source_target_pairs={{0,32},{16,48},{1,33},{17,49},{2,34},{18,50},{3,35},{19,51},{4,36}... | collective-permute-start | bytes 983048 | tf_op jit(solution)/shard_map/ppermute | solution.py:17
  20.5 7.5 %collective-permute-start.2 = (bf16[128,1280]{1,0:T(8,128)(2,1)S(1)}, bf16[128,1280]{1,0:T(8,128)(2,1)S(1)}, u32[]{:S(2)}, u32[]{:S(2)}) collective-permute-start(bf16[128,1280]{1,0:T(8,128)(2,1)S(1)} %broadcast_select_fusion.1), channel_id=1, source_target_pairs={{0,64},{16,80},{32,96},{48,112},{1,65},{17,81},{33,97},{49,113},{2... | collective-permute-start | bytes 983048 | tf_op jit(solution)/shard_map/ppermute | solution.py:17
  21.8 18.5 %copy-start.3 = (s32[8,16]{1,0:T(8,128)S(1)}, s32[8,16]{1,0:T(8,128)}, u32[]{:S(2)}) copy-start(s32[8,16]{1,0:T(8,128)} %param.14) | copy-start | bytes 1540
  41.2 24.6 %all-to-all-start = ((s32[128,1,128]{2,1,0:T(1,128)}), s32[128,1,128]{2,1,0:T(1,128)S(1)}, u32[]{:S(2)}, u32[]{:S(2)}) async-start(s32[128,1,128]{2,1,0:T(1,128)} %reshape.115), calls=%async_computation | async-start | bytes 131072 | tf_op jit(solution)/shard_map/all_to_all | solution.py:69
  133.6 10.3 %copy-start.5 = (f32[3,512]{1,0:T(4,128)S(1)}, f32[3,512]{1,0:T(4,128)}, u32[]{:S(2)}) copy-start(f32[3,512]{1,0:T(4,128)} %param.12) | copy-start | bytes 18436
  133.6 10.3 %copy-start.4 = (f32[8,512]{1,0:T(8,128)S(1)}, f32[8,512]{1,0:T(8,128)}, u32[]{:S(2)}) copy-start(f32[8,512]{1,0:T(8,128)} %param.11) | copy-start | bytes 49156
  133.6 10.3 %copy-start.6 = (s32[8]{0:T(128)S(1)}, s32[8]{0:T(128)}, u32[]{:S(2)}) copy-start(s32[8]{0:T(128)} %param.15) | copy-start | bytes 100
  133.6 10.4 %copy-start.2 = (f32[8,3,512]{2,0,1:T(8,128)S(1)}, f32[8,3,512]{2,0,1:T(8,128)}, u32[]{:S(2)}) copy-start(f32[8,3,512]{2,0,1:T(8,128)} %param.10) | copy-start | bytes 147460
  133.6 61.7 %all-to-all-start.1 = ((bf16[128,2,8192]{2,1,0:T(2,128)(2,1)}), bf16[128,2,8192]{2,1,0:T(2,128)(2,1)}, u32[]{:S(2)}, u32[]{:S(2)}) async-start(bf16[128,2,8192]{2,1,0:T(2,128)(2,1)} %reshape.107), calls=%async_computation.2 | async-start | bytes 8388608 | tf_op jit(solution)/shard_map/all_to_all | solution.py:102
  300.5 11.0 %copy-start.1 = (bf16[512,128]{1,0:T(8,128)(2,1)S(1)}, bf16[512,128]{1,0:T(8,128)(2,1)}, u32[]{:S(2)}) copy-start(bf16[512,128]{1,0:T(8,128)(2,1)} %param.13) | copy-start | bytes 393220
Sparse Core Ops, SparseCore 0:
  40.4 81.0 reduce-scatter.1
